TPU v7x, 32 devices: a whole 2x2x4 slice. The times are simulated.
32 devices in a mesh: groups: 2 (over y), pts: 4 (over z), cam: 4 (over x, core).
Axes of the slice: x: 2, y: 2, z: 4, core: 2. Of those that a mesh axis runs over, the one named last changes fastest.
Arguments:
- cam_jac: float32 [2, 9, 131072], P(None, None, ('groups', 'pts', 'cam')), parts along dimension 2, may hold values from -0.4 to 0.4
- point_jac: float32 [2, 3, 131072], P(None, None, ('groups', 'pts', 'cam')), parts along dimension 2, may hold values from -3 to 3
- obs_cam: int32 [131072], P(('groups', 'pts', 'cam')), parts along dimension 0, may hold values from 0 to 511
- obs_point: int32 [131072], P(('groups', 'pts', 'cam')), parts along dimension 0, may hold values from 0 to 4095
- point_damp: float32 [32768], P(('groups', 'pts')), parts along dimension 0, may hold values from 0.5 to 4
- cam_damp: float32 [4096], P(('groups', 'cam')), parts along dimension 0, may hold values from 0.5 to 4
- reduced_rhs: float32 [9, 4096], P(None, ('groups', 'cam')), parts along dimension 1, may hold values from -6 to 6
Outputs:
- solution: float32 [9, 4096], P(None, ('groups', 'cam')), parts along dimension 1
- residual: float32 [9, 4096], P(None, ('groups', 'cam')), parts along dimension 1
There are 2 independent parts, one for each index of `groups`. A program takes and returns all parts, laid end to end along the dimension named above; each array names one. Nothing has to cross between parts.
All inputs are finite; a program needn't handle non-finite values.
Results may differ from a plain program's by a relative error of at most 0.0003.
Values sent between devices are 32-bit elements; how exact they have to be, the bound alone decides.
No kernel may reach another device: no remote copies, remote signals or barrier semaphores. Data moves between devices by JAX's collectives and lax.ppermute only.
A program may use at most 64 MiB of HBM per device.

v0:
```python
import jax
import jax.numpy as jnp
from jax import lax
from jax.sharding import PartitionSpec as P

ITERS = 3
BF = jnp.bfloat16
F32 = jnp.float32


def split_of(count):
    lo = 1 << max(count.bit_length() - 1, 0) // 2
    while count % lo:
        lo //= 2
    return (count // lo, lo)


def pieces(value):
    first = lax.reduce_precision(value, exponent_bits=8, mantissa_bits=7)
    rest = value - first
    second = lax.reduce_precision(rest, exponent_bits=8, mantissa_bits=7)
    third = rest - second
    return (first.astype(BF), second.astype(BF), third.astype(BF))


class Index:

    def __init__(self, index, count):
        self.count = count
        self.hi, self.lo = split_of(count)
        high = index // self.lo
        low = index % self.lo
        hot = lax.broadcasted_iota(jnp.int32, (self.hi, index.shape[0]), 0) == high[None, :]
        self.hot = hot.astype(BF)
        self.hot3 = jnp.concatenate([self.hot] * 3, axis=1)
        self.hot3t = jnp.concatenate([self.hot] * 3, axis=0)
        self.low = lax.broadcasted_iota(jnp.int32, (self.lo, index.shape[0]), 0) == low[None, :]

    def segsum(self, terms):
        ncol = terms.shape[0]
        parts = [
            jnp.where(self.low[None], part[:, None, :], jnp.zeros((), BF)).reshape(
                ncol * self.lo, -1
            )
            for part in pieces(terms)
        ]
        spread = jnp.concatenate(parts, axis=1)
        out = lax.dot_general(
            self.hot3, spread, (((1,), (1,)), ((), ())), preferred_element_type=F32
        )
        return out.reshape(self.hi, ncol, self.lo).transpose(1, 0, 2).reshape(ncol, self.count)

    def gather(self, table):
        ncol = table.shape[0]
        mat = (
            table.reshape(ncol, self.hi, self.lo)
            .transpose(0, 2, 1)
            .reshape(ncol * self.lo, self.hi)
        )
        stacked = jnp.concatenate(pieces(mat), axis=1)
        spread = lax.dot_general(
            stacked, self.hot3t, (((1,), (0,)), ((), ())), preferred_element_type=F32
        ).reshape(ncol, self.lo, -1)
        return jnp.sum(jnp.where(self.low[None], spread, 0.0), axis=1)


def invert3(mat):
    c00 = mat[1, 1] * mat[2, 2] - mat[1, 2] * mat[2, 1]
    c01 = mat[0, 2] * mat[2, 1] - mat[0, 1] * mat[2, 2]
    c02 = mat[0, 1] * mat[1, 2] - mat[0, 2] * mat[1, 1]
    c10 = mat[1, 2] * mat[2, 0] - mat[1, 0] * mat[2, 2]
    c11 = mat[0, 0] * mat[2, 2] - mat[0, 2] * mat[2, 0]
    c12 = mat[0, 2] * mat[1, 0] - mat[0, 0] * mat[1, 2]
    c20 = mat[1, 0] * mat[2, 1] - mat[1, 1] * mat[2, 0]
    c21 = mat[0, 1] * mat[2, 0] - mat[0, 0] * mat[2, 1]
    c22 = mat[0, 0] * mat[1, 1] - mat[0, 1] * mat[1, 0]
    det = mat[0, 0] * c00 + mat[0, 1] * c10 + mat[0, 2] * c20
    adj = jnp.stack(
        [jnp.stack([c00, c01, c02]), jnp.stack([c10, c11, c12]), jnp.stack([c20, c21, c22])]
    )
    return adj / det


def normal_six(point_jac):
    pairs = [(0, 0), (0, 1), (0, 2), (1, 1), (1, 2), (2, 2)]
    return jnp.stack(
        [jnp.sum(point_jac[:, first] * point_jac[:, second], axis=0) for first, second in pairs]
    )


def expand_six(six):
    return jnp.stack(
        [
            jnp.stack([six[0], six[1], six[2]]),
            jnp.stack([six[1], six[3], six[4]]),
            jnp.stack([six[2], six[4], six[5]]),
        ]
    )


def point_inverse(six, damp):
    mat = expand_six(six) + damp[None, None, :] * jnp.eye(3, dtype=jnp.float32)[:, :, None]
    return invert3(mat)


def norm_sum(value):
    return lax.psum(value, "cam")


def on_device(cam_jac, point_jac, obs_cam, obs_point, point_damp, cam_damp, reduced_rhs):
    npts = point_damp.shape[0]
    ncam = reduced_rhs.shape[1]
    by_point = Index(obs_point, npts)
    by_cam = Index(obs_cam, ncam)
    six_terms = by_point.segsum(normal_six(point_jac))
    pshare = npts // lax.axis_size("cam")
    pstart = lax.axis_index("cam") * pshare
    six_share = lax.psum_scatter(six_terms, "cam", scatter_dimension=1, tiled=True)
    damp_pts = lax.dynamic_slice_in_dim(point_damp, pstart, pshare, 0)
    inv_share = point_inverse(six_share, damp_pts)
    diag_terms = by_cam.segsum(jnp.sum(cam_jac * cam_jac, axis=0))
    cam_diag = lax.psum(diag_terms, "pts") + cam_damp[None, :]
    solution = jnp.zeros_like(reduced_rhs)
    residual = reduced_rhs
    pre = residual / cam_diag
    direction = pre
    rz = norm_sum(jnp.sum(residual * pre))
    for step in range(ITERS):
        dir_obs = by_cam.gather(direction)
        y = jnp.sum(cam_jac * dir_obs[None], axis=1)
        reduced_u_part = by_point.segsum(jnp.sum(point_jac * y[:, None, :], axis=0))
        u_share = lax.psum_scatter(reduced_u_part, "cam", scatter_dimension=1, tiled=True)
        w_share = jnp.sum(inv_share * u_share[None, :, :], axis=1)
        w = lax.all_gather(w_share, "cam", axis=1, tiled=True)
        z = y - jnp.sum(point_jac * by_point.gather(w)[None], axis=1)
        image = cam_damp[None, :] * direction + lax.psum(
            by_cam.segsum(jnp.sum(cam_jac * z[:, None, :], axis=0)), "pts"
        )
        alpha = rz / lax.psum(jnp.sum(direction * image), "cam")
        solution = solution + alpha * direction
        residual = residual - alpha * image
        pre = residual / cam_diag
        new_rz = norm_sum(jnp.sum(residual * pre))
        direction = pre + new_rz / rz * direction
        rz = new_rz
    return (solution, residual)


def solution(mesh):
    return jax.shard_map(
        on_device,
        mesh=mesh,
        in_specs=(
            P(None, None, ("groups", "pts", "cam")),
            P(None, None, ("groups", "pts", "cam")),
            P(("groups", "pts", "cam")),
            P(("groups", "pts", "cam")),
            P(("groups", "pts")),
            P(("groups", "cam")),
            P(None, ("groups", "cam")),
        ),
        out_specs=(P(None, ("groups", "cam")), P(None, ("groups", "cam"))),
        check_vma=False,
    )
```

profile of v0, /device:TPU:0, one launch (start us, length us, event | category | flops | bytes accessed | tf_op | source)
XLA Modules:
  0.0 301.3 jit_solution(13803809787770061255)
XLA Ops:
  7.2 0.7 add_select_fusion.1
  7.9 0.7 add_select_fusion.3
  8.7 1.4 multiply_reduce_fusion.6
  10.6 1.1 fusion.24
  12.0 20.9 %psum.70 = f32[9,512]{1,0:T(8,128)S(1)} all-reduce(f32[9,512]{1,0:T(8,128)S(1)} %reshape.948), channel_id=1, replica_groups=mesh['groups'=2,'pts'=4,'cam'=4] {'pts'}, use_global_device_ids=true, to_apply=%region_1.2 | all-reduce | flops 4608 | bytes 36864 | tf_op jit(solution)/shard_map/psum | solution.py:122
  35.6 1.4 fusion.6
  37.1 2.9 copy.107
  40.5 0.9 broadcast_select_fusion.2
  41.4 3.0 %fusion = f32[64,384]{1,0:T(8,128)S(1)} fusion(bf16[384,4096]{1,0:T(8,128)(2,1)S(1)} %bitcast.157, bf16[384,4096]{1,0:T(8,128)(2,1)S(1)} %bitcast.156, bf16[384,4096]{1,0:T(8,128)(2,1)S(1)} %bitcast.155, bf16[64,4096]{1,0:T(8,128)(2,1)S(1)} %get-tuple-element.105), kind=kOutput, calls=%fused_computation | convolution fusion | flops 637009920 | bytes 10059776 | tf_op jit(solution)/shard_map/dot_general | solution.py:48
  44.6 0.7 reshape.953
  45.4 0.7 dynamic_slice.3
  46.2 23.4 %reduce-scatter.13.cloned.1.call-done = f32[1024,3]{1,0:T(8,128)} async-done(((f32[4096,3]{1,0:T(8,128)}), f32[1024,3]{1,0:T(8,128)}) %reduce-scatter.13.cloned.1.call-update) | async-done | bytes 12304
  69.5 1.2 copy.102
  70.8 20.9 %reduce-scatter.11.cloned.1.call-done = f32[6,1024]{1,0:T(8,128)} async-done(((f32[6,4096]{1,0:T(8,128)}), f32[6,1024]{1,0:T(8,128)}) %reduce-scatter.11.cloned.1.call-update) | async-done | bytes 24592 | tf_op jit(solution)/shard_map/reduce_scatter | solution.py:118
  91.6 0.8 fusion.120
  92.5 0.8 fusion.119
  93.4 0.8 slice_bitcast_fusion
  94.4 5.4 %all_gather.9 = f32[3,4096]{1,0:T(4,128)S(1)} all-gather(f32[3,1024]{1,0:T(4,128)S(1)} %get-tuple-element.16), channel_id=1, replica_groups=mesh['groups'=2,'pts'=4,'cam'=4] {'cam'}, dimensions={1}, use_global_device_ids=true | all-gather | bytes 61440 | tf_op jit(solution)/shard_map/all_gather | solution.py:134
  100.1 0.6 fusion.51
  102.1 1.1 fusion.30
  103.4 19.0 %psum.72 = f32[9,512]{1,0:T(8,128)S(1)} all-reduce(f32[9,512]{1,0:T(8,128)S(1)} %reshape.960), channel_id=1, replica_groups=mesh['groups'=2,'pts'=4,'cam'=4] {'pts'}, use_global_device_ids=true, to_apply=%region_19.20 | all-reduce | flops 4608 | bytes 36864 | tf_op jit(solution)/shard_map/psum | solution.py:136
  122.4 0.6 multiply_reduce_fusion.20
  123.0 6.6 %all-reduce = (f32[]{:T(128)}, f32[]{:T(128)}) all-reduce(f32[]{:T(128)} %get-tuple-element.9, f32[]{:T(128)} %get-tuple-element.8), channel_id=1, replica_groups=mesh['groups'=2,'pts'=4,'cam'=4] {'cam'}, use_global_device_ids=true, to_apply=%region_3.4 | all-reduce | flops 2 | bytes 16 | tf_op jit(solution)/shard_map/psum | solution.py:107
  131.0 0.6 multiply_reduce_fusion.19
  131.6 6.4 %psum.74 = f32[]{:T(128)} all-reduce(f32[]{:T(128)} %get-tuple-element.14), channel_id=1, replica_groups=mesh['groups'=2,'pts'=4,'cam'=4] {'cam'}, use_global_device_ids=true, to_apply=%region_23.24 | all-reduce | flops 1 | bytes 8 | tf_op jit(solution)/shard_map/psum | solution.py:107
  141.3 1.4 fusion.12
  142.8 2.9 copy.108
  145.8 29.0 %reduce-scatter.15.cloned.1.call-done = f32[1024,3]{1,0:T(8,128)} async-done(((f32[4096,3]{1,0:T(8,128)}), f32[1024,3]{1,0:T(8,128)}) %reduce-scatter.15.cloned.1.call-update) | async-done | bytes 12304
  174.8 1.2 copy.104
  176.1 5.2 %all_gather.10 = f32[3,4096]{1,0:T(4,128)S(1)} all-gather(f32[3,1024]{1,0:T(4,128)S(1)} %multiply_reduce_fusion.14), channel_id=1, replica_groups=mesh['groups'=2,'pts'=4,'cam'=4] {'cam'}, dimensions={1}, use_global_device_ids=true | all-gather | bytes 61440 | tf_op jit(solution)/shard_map/all_gather | solution.py:134
  181.6 0.6 fusion.50
  183.6 1.1 fusion.36
  184.9 19.0 %psum.75 = f32[9,512]{1,0:T(8,128)S(1)} all-reduce(f32[9,512]{1,0:T(8,128)S(1)} %reshape.970), channel_id=1, replica_groups=mesh['groups'=2,'pts'=4,'cam'=4] {'pts'}, use_global_device_ids=true, to_apply=%region_32.33 | all-reduce | flops 4608 | bytes 36864 | tf_op jit(solution)/shard_map/psum | solution.py:136
  203.9 0.6 multiply_reduce_fusion.18
  204.5 6.6 %psum.76 = f32[]{:T(128)} all-reduce(f32[]{:T(128)} %multiply_reduce_fusion.18), channel_id=1, replica_groups=mesh['groups'=2,'pts'=4,'cam'=4] {'cam'}, use_global_device_ids=true, to_apply=%region_34.35 | all-reduce | flops 1 | bytes 8 | tf_op jit(solution)/shard_map/psum | solution.py:139
  212.4 0.6 multiply_reduce_fusion.17
  213.0 6.6 %psum.77 = f32[]{:T(128)} all-reduce(f32[]{:T(128)} %get-tuple-element.12), channel_id=1, replica_groups=mesh['groups'=2,'pts'=4,'cam'=4] {'cam'}, use_global_device_ids=true, to_apply=%region_36.37 | all-reduce | flops 1 | bytes 8 | tf_op jit(solution)/shard_map/psum | solution.py:107
  223.0 1.4 fusion.18
  224.4 2.9 copy.109
  227.4 29.1 %reduce-scatter.17.cloned.1.call-done = f32[1024,3]{1,0:T(8,128)} async-done(((f32[4096,3]{1,0:T(8,128)}), f32[1024,3]{1,0:T(8,128)}) %reduce-scatter.17.cloned.1.call-update) | async-done | bytes 12304
  256.5 1.2 copy.106
  257.8 5.2 %all_gather.11 = f32[3,4096]{1,0:T(4,128)S(1)} all-gather(f32[3,1024]{1,0:T(4,128)S(1)} %multiply_reduce_fusion.13), channel_id=1, replica_groups=mesh['groups'=2,'pts'=4,'cam'=4] {'cam'}, dimensions={1}, use_global_device_ids=true | all-gather | bytes 61440 | tf_op jit(solution)/shard_map/all_gather | solution.py:134
  263.3 0.6 fusion.49
  265.3 1.1 fusion.42
  266.6 19.0 %psum.78 = f32[9,512]{1,0:T(8,128)S(1)} all-reduce(f32[9,512]{1,0:T(8,128)S(1)} %reshape.980), channel_id=1, replica_groups=mesh['groups'=2,'pts'=4,'cam'=4] {'pts'}, use_global_device_ids=true, to_apply=%region_45.46 | all-reduce | flops 4608 | bytes 36864 | tf_op jit(solution)/shard_map/psum | solution.py:136
  285.6 0.6 multiply_reduce_fusion.16
  286.2 6.6 %psum.79 = f32[]{:T(128)} all-reduce(f32[]{:T(128)} %multiply_reduce_fusion.16), channel_id=1, replica_groups=mesh['groups'=2,'pts'=4,'cam'=4] {'cam'}, use_global_device_ids=true, to_apply=%region_47.48 | all-reduce | flops 1 | bytes 8 | tf_op jit(solution)/shard_map/psum | solution.py:139
  294.1 0.6 multiply_subtract_fusion
  (103 shorter events, 14.1 us)
Async XLA Ops:
  7.2 62.4 %reduce-scatter.13.cloned.1.call-start = ((), (), s32[]{:S(2)}) async-start(), calls=%async_computation.5 | async-start | bytes 2621440
  10.6 22.2 %copy-start.2 = (f32[9,512]{1,0:T(8,128)S(1)}, f32[9,512]{1,0:T(8,128)}, u32[]{:S(2)}) copy-start(f32[9,512]{1,0:T(8,128)} %param.13) | copy-start | bytes 55300
  10.6 22.2 %copy-start.3 = (f32[512]{0:T(512)S(1)}, f32[512]{0:T(512)}, u32[]{:S(2)}) copy-start(f32[512]{0:T(512)} %param.12) | copy-start | bytes 6148
  33.6 1.0 copy-start
  33.7 1.1 copy-start.1
  40.0 51.6 %reduce-scatter.11.cloned.1.call-start = ((), (), s32[]{:S(2)}) async-start(), calls=%async_computation.4 | async-start | bytes 163840 | tf_op jit(solution)/shard_map/reduce_scatter | solution.py:118
  45.4 129.4 %reduce-scatter.15.cloned.1.call-start = ((), (), s32[]{:S(2)}) async-start(), calls=%async_computation.6 | async-start | bytes 2621440
  145.7 110.8 %reduce-scatter.17.cloned.1.call-start = ((), (), s32[]{:S(2)}) async-start(), calls=%async_computation.7 | async-start | bytes 2621440
Sparse Core Ops, SparseCore 0:
  40.2 29.3 reduce-scatter.12
  72.0 19.6 reduce-scatter.10
  145.8 28.8 reduce-scatter.14
  227.5 28.9 reduce-scatter.16
where the time goes:
time: 302 us; the launch traced here: 301 us
  blocking collectives  126 us (42%)
  waiting for transfers between devices  102 us (34%)
  between operations  21.1 us (7%)
  local copies, waits for them, and re-layouts  19.2 us (6%)
  other arithmetic  16.9 us (6%)
  matrix products  15 us (5%)
    unnamed x7, waiting for transfers between devices  81.6 us
    psum x3, blocking collectives, on_device(): lax.psum(by_cam.segsum(jnp.sum(cam_jac * z[:, None, :], axis=0)), 'pts')  56.9 us
    reduce_scatter x1, waiting for transfers between devices, on_device(): lax.psum_scatter(six_terms, 'cam', scatter_dimension=1, tiled=True)  20.9 us
    psum x1, blocking collectives, on_device(): cam_diag = lax.psum(diag_terms, 'pts') + cam_damp[None, :]  20.9 us
    psum x3, blocking collectives, norm_sum(): return lax.psum(value, 'cam')  19.5 us
    all_gather x3, blocking collectives, on_device(): w = lax.all_gather(w_share, 'cam', axis=1, tiled=True)  15.9 us
    psum x2, blocking collectives, on_device(): alpha = rz / lax.psum(jnp.sum(direction * image), 'cam')  13.1 us
    unnamed x14, local copies, waits for them, and re-layouts  13 us
  transfers between devices with their start and end apart: 4, of which 4 were waited for; matrix products, arithmetic and copies ran while one was open for 2% of the time, Pallas kernels for 0%

commit v1 on v0

--- a/solution.py
+++ b/solution.py
@@ -1,3 +1,4 @@
+import functools
 import jax
 import jax.numpy as jnp
 from jax import lax
@@ -6,6 +7,14 @@
 ITERS = 3
 BF = jnp.bfloat16
 F32 = jnp.float32
+
+
+def _spread_spots(here_x, bus_axis):
+    moved = jnp.sum(lax.all_gather(here_x, bus_axis), axis=0)
+    return moved
+
+
+shape_the_lanes = functools.partial(_spread_spots, bus_axis="pts")
 
 
 def split_of(count):
@@ -133,8 +142,8 @@
         w_share = jnp.sum(inv_share * u_share[None, :, :], axis=1)
         w = lax.all_gather(w_share, "cam", axis=1, tiled=True)
         z = y - jnp.sum(point_jac * by_point.gather(w)[None], axis=1)
-        image = cam_damp[None, :] * direction + lax.psum(
-            by_cam.segsum(jnp.sum(cam_jac * z[:, None, :], axis=0)), "pts"
+        image = cam_damp[None, :] * direction + shape_the_lanes(
+            by_cam.segsum(jnp.sum(cam_jac * z[:, None, :], axis=0))
         )
         alpha = rz / lax.psum(jnp.sum(direction * image), "cam")
         solution = solution + alpha * direction

time: 302 us -> 291 us (0.964)
  blocking collectives: 126 us -> 110 us
  waiting for transfers between devices: 102 us -> 108 us
    psum x3 -> x0, blocking collectives: 56.9 us -> none  [on_device(): lax.psum(by_cam.segsum(jnp.sum(cam_jac * z[:, None, :], axis=0)), 'pts')]
    all_gather x0 -> x3, blocking collectives: none -> 40.5 us  [_spread_spots(): moved = jnp.sum(lax.all_gather(here_x, bus_axis), axis=0)]
    unnamed x7, waiting for transfers between devices: 81.6 us -> 87.3 us
where the time goes in v1:
time: 291 us; the launch traced here: 290 us
  blocking collectives  110 us (38%)
  waiting for transfers between devices  108 us (37%)
  between operations  21.1 us (7%)
  local copies, waits for them, and re-layouts  19.2 us (7%)
  other arithmetic  17 us (6%)
  matrix products  15 us (5%)
    unnamed x7, waiting for transfers between devices  87.3 us
    all_gather x3, blocking collectives, _spread_spots(): moved = jnp.sum(lax.all_gather(here_x, bus_axis), axis=0)  40.5 us
    reduce_scatter x1, waiting for transfers between devices, on_device(): lax.psum_scatter(six_terms, 'cam', scatter_dimension=1, tiled=True)  20.9 us
    psum x1, blocking collectives, on_device(): cam_diag = lax.psum(diag_terms, 'pts') + cam_damp[None, :]  20.8 us
    psum x3, blocking collectives, norm_sum(): return lax.psum(value, 'cam')  19.5 us
    all_gather x3, blocking collectives, on_device(): w = lax.all_gather(w_share, 'cam', axis=1, tiled=True)  15.9 us
    psum x2, blocking collectives, on_device(): alpha = rz / lax.psum(jnp.sum(direction * image), 'cam')  13.1 us
    unnamed x14, local copies, waits for them, and re-layouts  13 us
  transfers between devices with their start and end apart: 4, of which 4 were waited for; matrix products, arithmetic and copies ran while one was open for 2% of the time, Pallas kernels for 0%

profile of v1, /device:TPU:0, one launch (start us, length us, event | category | flops | bytes accessed | tf_op | source)
XLA Modules:
  0.0 290.4 jit_solution(11457569639600192446)
XLA Ops:
  7.2 0.7 add_select_fusion.1
  7.9 0.7 add_select_fusion.3
  8.7 1.4 multiply_reduce_fusion.6
  10.7 1.1 fusion.24
  12.0 20.8 %psum.49 = f32[9,512]{1,0:T(8,128)S(1)} all-reduce(f32[9,512]{1,0:T(8,128)S(1)} %reshape.939), channel_id=1, replica_groups=mesh['groups'=2,'pts'=4,'cam'=4] {'pts'}, use_global_device_ids=true, to_apply=%region_1.2 | all-reduce | flops 4608 | bytes 36864 | tf_op jit(solution)/shard_map/psum | solution.py:131
  35.6 1.4 fusion.6
  37.0 2.9 %copy.104 = f32[3,64,64]{0,2,1:T(8,128)} copy(f32[3,64,64]{1,2,0:T(8,128)S(1)} %bitcast.189) | data formatting | bytes 98304
  40.5 0.9 broadcast_select_fusion.2
  41.4 3.0 %fusion = f32[64,384]{1,0:T(8,128)S(1)} fusion(bf16[384,4096]{1,0:T(8,128)(2,1)S(1)} %bitcast.157, bf16[384,4096]{1,0:T(8,128)(2,1)S(1)} %bitcast.156, bf16[384,4096]{1,0:T(8,128)(2,1)S(1)} %bitcast.155, bf16[64,4096]{1,0:T(8,128)(2,1)S(1)} %get-tuple-element.105), kind=kOutput, calls=%fused_computation | convolution fusion | flops 637009920 | bytes 10059776 | tf_op jit(solution)/shard_map/dot_general | solution.py:57
  44.6 0.7 reshape.944
  45.4 0.7 dynamic_slice.3
  46.1 23.5 %reduce-scatter.13.cloned.1.call-done = f32[1024,3]{1,0:T(8,128)} async-done(((f32[4096,3]{1,0:T(8,128)}), f32[1024,3]{1,0:T(8,128)}) %reduce-scatter.13.cloned.1.call-update) | async-done | bytes 12304
  69.5 1.2 copy.99
  70.8 20.9 %reduce-scatter.11.cloned.1.call-done = f32[6,1024]{1,0:T(8,128)} async-done(((f32[6,4096]{1,0:T(8,128)}), f32[6,1024]{1,0:T(8,128)}) %reduce-scatter.11.cloned.1.call-update) | async-done | bytes 24592 | tf_op jit(solution)/shard_map/reduce_scatter | solution.py:127
  91.6 0.8 fusion.120
  92.5 0.8 fusion.119
  93.4 0.8 slice_bitcast_fusion
  94.4 5.4 %all_gather.18 = f32[3,4096]{1,0:T(4,128)S(1)} all-gather(f32[3,1024]{1,0:T(4,128)S(1)} %get-tuple-element.16), channel_id=1, replica_groups=mesh['groups'=2,'pts'=4,'cam'=4] {'cam'}, dimensions={1}, use_global_device_ids=true | all-gather | bytes 61440 | tf_op jit(solution)/shard_map/all_gather | solution.py:143
  100.1 0.6 fusion.51
  102.1 1.1 fusion.30
  103.4 13.5 %all_gather.19 = f32[4,9,512]{2,1,0:T(8,128)S(1)} all-gather(f32[1,9,512]{2,1,0:T(8,128)S(1)} %all_gather_reshape.9), channel_id=1, replica_groups=mesh['groups'=2,'pts'=4,'cam'=4] {'pts'}, dimensions={0}, use_global_device_ids=true | all-gather | bytes 92160 | tf_op jit(solution)/shard_map/all_gather | solution.py:13
  117.0 0.6 multiply_reduce_fusion.20
  117.6 6.6 %all-reduce = (f32[]{:T(128)}, f32[]{:T(128)}) all-reduce(f32[]{:T(128)} %get-tuple-element.9, f32[]{:T(128)} %get-tuple-element.8), channel_id=1, replica_groups=mesh['groups'=2,'pts'=4,'cam'=4] {'cam'}, use_global_device_ids=true, to_apply=%region_3.4 | all-reduce | flops 2 | bytes 16 | tf_op jit(solution)/shard_map/psum | solution.py:116
  125.5 0.6 multiply_reduce_fusion.19
  126.1 6.4 %psum.52 = f32[]{:T(128)} all-reduce(f32[]{:T(128)} %get-tuple-element.14), channel_id=1, replica_groups=mesh['groups'=2,'pts'=4,'cam'=4] {'cam'}, use_global_device_ids=true, to_apply=%region_23.24 | all-reduce | flops 1 | bytes 8 | tf_op jit(solution)/shard_map/psum | solution.py:116
  135.8 1.4 fusion.12
  137.3 2.9 %copy.105 = f32[3,64,64]{0,2,1:T(8,128)} copy(f32[3,64,64]{1,2,0:T(8,128)S(1)} %bitcast.190) | data formatting | bytes 98304
  140.3 31.8 %reduce-scatter.15.cloned.1.call-done = f32[1024,3]{1,0:T(8,128)} async-done(((f32[4096,3]{1,0:T(8,128)}), f32[1024,3]{1,0:T(8,128)}) %reduce-scatter.15.cloned.1.call-update) | async-done | bytes 12304
  172.1 1.2 copy.101
  173.4 5.2 %all_gather.20 = f32[3,4096]{1,0:T(4,128)S(1)} all-gather(f32[3,1024]{1,0:T(4,128)S(1)} %multiply_reduce_fusion.14), channel_id=1, replica_groups=mesh['groups'=2,'pts'=4,'cam'=4] {'cam'}, dimensions={1}, use_global_device_ids=true | all-gather | bytes 61440 | tf_op jit(solution)/shard_map/all_gather | solution.py:143
  178.9 0.6 fusion.50
  180.9 1.1 fusion.36
  182.2 13.5 %all_gather.21 = f32[4,9,512]{2,1,0:T(8,128)S(1)} all-gather(f32[1,9,512]{2,1,0:T(8,128)S(1)} %all_gather_reshape.10), channel_id=1, replica_groups=mesh['groups'=2,'pts'=4,'cam'=4] {'pts'}, dimensions={0}, use_global_device_ids=true | all-gather | bytes 92160 | tf_op jit(solution)/shard_map/all_gather | solution.py:13
  195.7 0.6 multiply_reduce_fusion.18
  196.3 6.6 %psum.53 = f32[]{:T(128)} all-reduce(f32[]{:T(128)} %multiply_reduce_fusion.18), channel_id=1, replica_groups=mesh['groups'=2,'pts'=4,'cam'=4] {'cam'}, use_global_device_ids=true, to_apply=%region_34.35 | all-reduce | flops 1 | bytes 8 | tf_op jit(solution)/shard_map/psum | solution.py:148
  204.2 0.6 multiply_reduce_fusion.17
  204.8 6.6 %psum.54 = f32[]{:T(128)} all-reduce(f32[]{:T(128)} %get-tuple-element.12), channel_id=1, replica_groups=mesh['groups'=2,'pts'=4,'cam'=4] {'cam'}, use_global_device_ids=true, to_apply=%region_36.37 | all-reduce | flops 1 | bytes 8 | tf_op jit(solution)/shard_map/psum | solution.py:116
  214.8 1.4 fusion.18
  216.3 2.9 %copy.106 = f32[3,64,64]{0,2,1:T(8,128)} copy(f32[3,64,64]{1,2,0:T(8,128)S(1)} %bitcast.191) | data formatting | bytes 98304
  219.2 31.9 %reduce-scatter.17.cloned.1.call-done = f32[1024,3]{1,0:T(8,128)} async-done(((f32[4096,3]{1,0:T(8,128)}), f32[1024,3]{1,0:T(8,128)}) %reduce-scatter.17.cloned.1.call-update) | async-done | bytes 12304
  251.2 1.2 copy.103
  252.4 5.2 %all_gather.22 = f32[3,4096]{1,0:T(4,128)S(1)} all-gather(f32[3,1024]{1,0:T(4,128)S(1)} %multiply_reduce_fusion.13), channel_id=1, replica_groups=mesh['groups'=2,'pts'=4,'cam'=4] {'cam'}, dimensions={1}, use_global_device_ids=true | all-gather | bytes 61440 | tf_op jit(solution)/shard_map/all_gather | solution.py:143
  257.9 0.6 fusion.49
  259.9 1.1 fusion.42
  261.2 13.5 %all_gather.23 = f32[4,9,512]{2,1,0:T(8,128)S(1)} all-gather(f32[1,9,512]{2,1,0:T(8,128)S(1)} %all_gather_reshape.11), channel_id=1, replica_groups=mesh['groups'=2,'pts'=4,'cam'=4] {'pts'}, dimensions={0}, use_global_device_ids=true | all-gather | bytes 92160 | tf_op jit(solution)/shard_map/all_gather | solution.py:13
  274.7 0.6 multiply_reduce_fusion.16
  275.4 6.6 %psum.55 = f32[]{:T(128)} all-reduce(f32[]{:T(128)} %multiply_reduce_fusion.16), channel_id=1, replica_groups=mesh['groups'=2,'pts'=4,'cam'=4] {'cam'}, use_global_device_ids=true, to_apply=%region_47.48 | all-reduce | flops 1 | bytes 8 | tf_op jit(solution)/shard_map/psum | solution.py:148
  283.3 0.6 multiply_subtract_fusion
  (106 shorter events, 14.2 us)
Async XLA Ops:
  7.2 62.4 %reduce-scatter.13.cloned.1.call-start = ((), (), s32[]{:S(2)}) async-start(), calls=%async_computation.5 | async-start | bytes 2621440
  10.6 22.2 %copy-start.2 = (f32[9,512]{1,0:T(8,128)S(1)}, f32[9,512]{1,0:T(8,128)}, u32[]{:S(2)}) copy-start(f32[9,512]{1,0:T(8,128)} %param.13) | copy-start | bytes 55300
  10.6 22.2 %copy-start.3 = (f32[512]{0:T(512)S(1)}, f32[512]{0:T(512)}, u32[]{:S(2)}) copy-start(f32[512]{0:T(512)} %param.12) | copy-start | bytes 6148
  33.6 1.0 copy-start
  33.6 1.1 copy-start.1
  40.0 51.6 %reduce-scatter.11.cloned.1.call-start = ((), (), s32[]{:S(2)}) async-start(), calls=%async_computation.4 | async-start | bytes 163840 | tf_op jit(solution)/shard_map/reduce_scatter | solution.py:127
  45.3 126.8 %reduce-scatter.15.cloned.1.call-start = ((), (), s32[]{:S(2)}) async-start(), calls=%async_computation.6 | async-start | bytes 2621440
  140.2 110.9 %reduce-scatter.17.cloned.1.call-start = ((), (), s32[]{:S(2)}) async-start(), calls=%async_computation.7 | async-start | bytes 2621440
Sparse Core Ops, SparseCore 0:
  40.1 29.3 reduce-scatter.12
  72.0 19.6 reduce-scatter.10
  140.4 31.6 reduce-scatter.14
  219.3 31.7 reduce-scatter.16
